TPU v7x, 32 devices: a whole 2x2x4 slice. The times are simulated.
32 devices in a mesh: band: 2 (over x), spk: 16 (over z, y, core).
Axes of the slice: x: 2, y: 2, z: 4, core: 2. Of those that a mesh axis runs over, the one named last changes fastest.
Arguments:
- direction: float32 [64, 128, 128], P(('band', 'spk')), parts along dimension 0, may hold values from -6 to 6
- plant: bfloat16 [832, 2, 128, 128], P(('band', 'spk')), parts along dimension 0
- tile_pairs: int32 [832, 2], P(('band', 'spk')), parts along dimension 0, may hold values from 0 to 127, as said below
- mic_weight: float32 [2, 128, 128], P('band', 'spk'), parts along dimension 0, may hold values from 0.3 to 3
Outputs:
- hessian_vector: float32 [64, 128, 128], P(('band', 'spk')), parts along dimension 0
There are 2 independent parts, one for each index of `band`. A program takes and returns all parts, laid end to end along the dimension named above; each array names one. Nothing has to cross between parts.
Inputs may be any that keep to these rules, and one draw needn't show every extreme that they name: `tile_pairs`: column 0 is a speaker block, column 1 a microphone block. The rows of one device (aligned blocks of 26 rows) all lie in that device's bin, and their speaker blocks s satisfy s // 2 = (device index) % 16; no pair repeats on a device. Counting microphone blocks m by the device m * 16 // 128, at most 4 rows of one device fall to any one device, and in every part one device gets exactly 4 from every device.
All inputs are finite; a program needn't handle non-finite values.
Results may differ from a plain program's by a relative error of at most 0.0032.
Values may be sent and summed in bfloat16 or wider, within the bound.
No kernel may reach another device: no remote copies, remote signals or barrier semaphores. Data moves between devices by JAX's collectives and lax.ppermute only.
A program may use at most 128 MiB of HBM per device.

v0:
```python
import jax
import jax.numpy as jnp
from jax import lax
from jax.sharding import PartitionSpec as P

SBLK = 32
MBLK = 128
SPEAKERS = 4096
reg_weight = 0.25


def complex_forward(plant, field_rows):
    halfway = field_rows.shape[-1] // 2
    product = jnp.einsum("tcij,tjk->tcik", plant, field_rows, preferred_element_type=jnp.float32)
    real_part = product[:, 0, :, :halfway] - product[:, 1, :, halfway:]
    imag_part = product[:, 0, :, halfway:] + product[:, 1, :, :halfway]
    return jnp.concatenate([real_part, imag_part], axis=-1)


def complex_adjoint(plant, field_rows):
    halfway = field_rows.shape[-1] // 2
    product = jnp.einsum("tcij,tik->tcjk", plant, field_rows, preferred_element_type=jnp.float32)
    real_part = product[:, 0, :, :halfway] + product[:, 1, :, halfway:]
    imag_part = product[:, 0, :, halfway:] - product[:, 1, :, :halfway]
    return jnp.concatenate([real_part, imag_part], axis=-1)


def per_device(direction, plant, tile_pairs, mic_weight):
    devices = lax.axis_size("spk")
    device_id = lax.axis_index("spk")
    unit_count = direction.shape[0]
    tile_count = plant.shape[0]
    block_size = direction.shape[1]
    field_width = direction.shape[2]
    groups_per_bin = SBLK // unit_count
    bin_count = devices // groups_per_bin
    peer_blocks = MBLK // devices
    mic_units = bin_count * peer_blocks
    my_bin = device_id // groups_per_bin
    local_unit = tile_pairs[:, 0] % unit_count
    mic_block = tile_pairs[:, 1]
    direction_rows = direction.astype(jnp.bfloat16)[local_unit]
    partial_field = complex_forward(plant, direction_rows)
    local_power = jnp.sum(jnp.square(plant.astype(jnp.float32)))
    power_terms = jnp.where(jnp.arange(bin_count) == my_bin, local_power, 0.0)
    bin_power = lax.psum(power_terms, "spk")
    weights_flat = mic_weight.reshape(mic_units, block_size)
    capacity = max(3, (2 * tile_count + devices - 1) // devices)
    target_peer = mic_block // peer_blocks
    peer_onehot = (target_peer[:, None] == jnp.arange(devices)[None, :]).astype(jnp.int32)
    running = jnp.cumsum(peer_onehot, axis=0)
    slot_rank = jnp.take_along_axis(running, target_peer[:, None], axis=1)[:, 0] - 1
    position = target_peer * capacity + slot_rank
    target_label = my_bin * peer_blocks + mic_block - target_peer * peer_blocks
    outgoing = (
        jnp.zeros((devices * capacity, block_size, field_width), jnp.float32)
        .at[position]
        .set(partial_field)
    )
    labels = jnp.full((devices * capacity,), mic_units, jnp.int32).at[position].set(target_label)
    labels_in = lax.all_to_all(
        labels.reshape(devices, capacity), "spk", split_axis=0, concat_axis=0, tiled=True
    )
    arrived = lax.all_to_all(
        outgoing.reshape(devices, capacity, block_size, field_width),
        "spk",
        split_axis=0,
        concat_axis=0,
        tiled=True,
    )
    flat_labels = labels_in.reshape(devices * capacity)
    pressure = jax.ops.segment_sum(
        arrived.reshape(devices * capacity, block_size, field_width),
        flat_labels,
        num_segments=mic_units + 1,
    )[:mic_units]
    weighted = (weights_flat[:, :, None] * pressure).astype(jnp.bfloat16)
    clipped = jnp.minimum(flat_labels, mic_units - 1)
    reply = weighted[clipped].reshape(devices, capacity, block_size, field_width)
    returned = lax.all_to_all(reply, "spk", split_axis=0, concat_axis=0, tiled=True)
    tile_weighted = returned.reshape(devices * capacity, block_size, field_width)[position]
    back_field = complex_adjoint(plant, tile_weighted)
    unit_onehot = (local_unit[:, None] == jnp.arange(unit_count)[None, :]).astype(jnp.float32)
    gram = jnp.einsum("tu,tjk->ujk", unit_onehot, back_field, precision=lax.Precision.HIGHEST)
    my_power = bin_power[my_bin]
    return gram + reg_weight * my_power / SPEAKERS * direction


def solution(mesh):
    placed = (
        P(("band", "spk"), None, None),
        P(("band", "spk"), None, None, None),
        P(("band", "spk"), None),
        P("band", "spk", None),
    )
    return jax.shard_map(
        per_device,
        mesh=mesh,
        in_specs=placed,
        out_specs=P(("band", "spk"), None, None),
        check_vma=False,
    )
```

profile of v0, /device:TPU:16, one launch (start us, length us, event | category | flops | bytes accessed | tf_op | source)
XLA Modules:
  0.0 212.3 jit_solution(8495858670104442344)
XLA Ops:
  0.0 0.0 copy-start
  0.0 0.8 fusion.16
  0.9 0.7 fusion.18
  1.5 0.1 fusion.9
  1.7 0.8 gather_fusion.3
  2.5 0.7 scatter_custom_fusion
  3.2 0.7 all_to_all.12
  3.9 6.2 %all-to-all-start = ((s32[16,1,4]{2,1,0:T(1,128)}), s32[16,1,4]{2,1,0:T(1,128)S(1)}, u32[]{:S(2)}, u32[]{:S(2)}) async-start(s32[16,1,4]{2,1,0:T(1,128)} %bitcast.10), calls=%async_computation | async-start | bytes 16384 | tf_op jit(solution)/shard_map/all_to_all | solution.py:61
  10.0 0.9 convert_element_type.14
  11.0 0.7 gather_fusion
  11.7 0.0 copy-done
  11.7 0.7 convolution_bitcast_fusion.1
  12.4 0.1 fusion.3
  12.5 0.1 fusion.5
  12.6 0.2 pad_maximum_fusion
  12.8 1.7 copy.38
  14.5 0.0 copy-start.1
  14.5 2.4 %broadcast_in_dim.9 = f32[64,128,128]{2,1,0:T(8,128)} broadcast(f32[]{:T(128)} %constant.79.clone.1), dimensions={} | broadcast | bytes 4194308 | tf_op jit(solution)/shard_map/broadcast_in_dim | solution.py:56
  16.9 0.0 copy-done.1
  16.9 5.4 %scatter_fusion = f32[64,128,128]{2,1,0:T(8,128)} fusion(f32[64,128,128]{2,1,0:T(8,128)} %broadcast_in_dim.9, s32[26]{0:T(128)S(1)} %fusion.15, f32[26,128,128]{2,1,0:T(8,128)S(1)} %copy-done.1), kind=kCustom, calls=%fused_computation.5 | custom fusion | bytes 5111912 | tf_op jit(solution)/shard_map/scatter | solution.py:58
  22.3 0.0 all-to-all-done
  22.3 6.0 %all-to-all-start.1 = ((f32[16,4,128,128]{3,2,1,0:T(8,128)}), f32[16,4,128,128]{3,2,1,0:T(8,128)}, u32[]{:S(2)}, u32[]{:S(2)}) async-start(f32[16,4,128,128]{3,2,1,0:T(8,128)} %bitcast.87), calls=%async_computation.1 | async-start | bytes 8388608 | tf_op jit(solution)/shard_map/all_to_all | solution.py:64
  28.3 0.5 broadcast.181
  28.9 0.7 minimum_reduce_fusion
  29.6 0.1 reshape.124
  29.6 0.1 reshape.132
  29.8 91.2 %all-to-all-done.1 = f32[16,4,128,128]{3,2,1,0:T(8,128)} async-done(((f32[16,4,128,128]{3,2,1,0:T(8,128)}), f32[16,4,128,128]{3,2,1,0:T(8,128)}, u32[]{:S(2)}, u32[]{:S(2)}) %all-to-all-start.1) | async-done | bytes 4194336 | tf_op jit(solution)/shard_map/all_to_all | solution.py:64
  121.1 0.0 copy-start.3
  121.1 8.8 %scatter_fusion.1 = f32[9,128,128]{2,1,0:T(8,128)S(1)} fusion(f32[9,128,128]{2,1,0:T(8,128)S(1)} %broadcast_in_dim.8, s32[64]{0:T(128)S(1)} %reshape.124, f32[64,128,128]{2,1,0:T(8,128)} %bitcast.17), kind=kCustom, calls=%fused_computation.6 | custom fusion | flops 1048576 | bytes 12583168 | tf_op jit(solution)/shard_map/scatter-add | solution.py:72
  129.9 0.0 copy-done.3
  129.9 0.2 fusion.8
  130.1 2.1 gather_fusion.1
  132.2 4.6 %all-to-all-start.2 = ((bf16[16,4,128,128]{3,2,1,0:T(8,128)(2,1)}), bf16[16,4,128,128]{3,2,1,0:T(8,128)(2,1)}, u32[]{:S(2)}, u32[]{:S(2)}) async-start(bf16[16,4,128,128]{3,2,1,0:T(8,128)(2,1)} %bitcast.88), calls=%async_computation.2 | async-start | bytes 4194304 | tf_op jit(solution)/shard_map/all_to_all | solution.py:80
  136.8 1.5 multiply_reduce_fusion
  138.9 64.1 %psum.7 = f32[1]{0:T(128)} all-reduce(f32[1]{0:T(128)} %bitcast.25), channel_id=1, replica_groups=mesh['band'=2,'spk'=16] {'spk'}, use_global_device_ids=true, to_apply=%region_5.6 | all-reduce | flops 1 | bytes 8 | tf_op jit(solution)/shard_map/psum | solution.py:46
  203.7 0.0 all-to-all-done.2
  203.7 2.3 %gather_fusion.2 = bf16[26,128,128]{2,1,0:T(8,128)(2,1)S(1)} fusion(bf16[64,128,128]{2,1,0:T(8,128)(2,1)} %bitcast.20, s32[1024]{0:T(1024)S(1)} %pad_clamp_fusion), kind=kCustom, calls=%fused_computation.2 | custom fusion | bytes 1704040 | tf_op jit(solution)/shard_map/gather | solution.py:81
  206.0 0.7 convolution_bitcast_fusion
  206.7 0.1 fusion
  206.8 0.1 fusion.2
  206.9 0.1 pad_maximum_fusion.1
  207.0 0.0 copy-start.2
  207.1 2.2 %copy.42 = f32[26,128,128]{2,0,1:T(8,128)} copy(f32[26,128,128]{1,2,0:T(8,128)S(1)} %pad_maximum_fusion.1) | data formatting | bytes 3407872 | tf_op jit(solution)/shard_map/concatenate | solution.py:25
  209.3 2.4 %fusion.10 = f32[2,128,128]{2,0,1:T(2,128)S(1)} fusion(f32[26,128,128]{2,0,1:T(8,128)} %copy.42, s32[26]{0:T(128)S(1)} %bitcast.90), kind=kOutput, calls=%fused_computation.41 | convolution fusion | flops 10223668 | bytes 1835112 | tf_op jit(solution)/shard_map/tu,tjk->ujk/dot_general | solution.py:84
  211.6 0.0 copy-done.2
  211.6 0.7 copy_add_fusion
  (10 shorter events, 0.1 us)
Async XLA Ops:
  0.0 11.7 %copy-start = (bf16[26,2,128,128]{3,2,1,0:T(8,128)(2,1)S(1)}, bf16[26,2,128,128]{3,2,1,0:T(8,128)(2,1)}, u32[]{:S(2)}) copy-start(bf16[26,2,128,128]{3,2,1,0:T(8,128)(2,1)} %param.5) | copy-start | bytes 5111812
  3.9 18.5 %all-to-all-start = ((s32[16,1,4]{2,1,0:T(1,128)}), s32[16,1,4]{2,1,0:T(1,128)S(1)}, u32[]{:S(2)}, u32[]{:S(2)}) async-start(s32[16,1,4]{2,1,0:T(1,128)} %bitcast.10), calls=%async_computation | async-start | bytes 16384 | tf_op jit(solution)/shard_map/all_to_all | solution.py:61
  14.5 2.4 %copy-start.1 = (f32[26,128,128]{2,1,0:T(8,128)S(1)}, f32[26,128,128]{2,1,0:T(8,128)}, u32[]{:S(2)}) copy-start(f32[26,128,128]{2,1,0:T(8,128)} %copy.38) | copy-start | bytes 5111812
  22.3 98.7 %all-to-all-start.1 = ((f32[16,4,128,128]{3,2,1,0:T(8,128)}), f32[16,4,128,128]{3,2,1,0:T(8,128)}, u32[]{:S(2)}, u32[]{:S(2)}) async-start(f32[16,4,128,128]{3,2,1,0:T(8,128)} %bitcast.87), calls=%async_computation.1 | async-start | bytes 8388608 | tf_op jit(solution)/shard_map/all_to_all | solution.py:64
  121.1 8.8 %copy-start.3 = (f32[1,8,128]{2,1,0:T(8,128)S(1)}, f32[1,8,128]{2,1,0:T(8,128)}, u32[]{:S(2)}) copy-start(f32[1,8,128]{2,1,0:T(8,128)} %param.7) | copy-start | bytes 12292
  132.2 71.5 %all-to-all-start.2 = ((bf16[16,4,128,128]{3,2,1,0:T(8,128)(2,1)}), bf16[16,4,128,128]{3,2,1,0:T(8,128)(2,1)}, u32[]{:S(2)}, u32[]{:S(2)}) async-start(bf16[16,4,128,128]{3,2,1,0:T(8,128)(2,1)} %bitcast.88), calls=%async_computation.2 | async-start | bytes 4194304 | tf_op jit(solution)/shard_map/all_to_all | solution.py:80
  207.0 4.6 %copy-start.2 = (f32[2,128,128]{2,1,0:T(8,128)S(1)}, f32[2,128,128]{2,1,0:T(8,128)}, u32[]{:S(2)}) copy-start(f32[2,128,128]{2,1,0:T(8,128)} %param.4) | copy-start | bytes 393220
where the time goes:
time: 213 us; the launch traced here: 212 us
  waiting for transfers between devices  91.3 us (43%)
  blocking collectives  64.1 us (30%)
  local copies, waits for them, and re-layouts  19.7 us (9%)
  starting transfers between devices  16.8 us (8%)
  other arithmetic  15.2 us (7%)
  matrix products  3.66 us (2%)
    all_to_all x1, waiting for transfers between devices, per_device(): lax.all_to_all(outgoing.reshape(devices, capacity, block_size, field_widt...  91.2 us
    psum x1, blocking collectives, per_device(): bin_power = lax.psum(power_terms, 'spk')  64.1 us
    scatter-add x1, other arithmetic, per_device(): jax.ops.segment_sum(arrived.reshape(devices * capacity, block_size, field...  8.78 us
    all_to_all x1, starting transfers between devices, per_device(): lax.all_to_all(labels.reshape(devices, capacity), 'spk', split_axis=0, co...  6.18 us
    all_to_all x1, starting transfers between devices, per_device(): lax.all_to_all(outgoing.reshape(devices, capacity, block_size, field_widt...  6.01 us
    scatter x1, local copies, waits for them, and re-layouts, per_device(): outgoing = jnp.zeros((devices * capacity, block_size, field_width), jnp.f...  5.43 us
    all_to_all x1, starting transfers between devices, per_device(): lax.all_to_all(reply, 'spk', split_axis=0, concat_axis=0, tiled=True)  4.59 us
  transfers between devices with their start and end apart: 3, of which 1 were waited for; matrix products, arithmetic and copies ran while one was open for 7% of the time, Pallas kernels for 0%

commit v1 on v0

--- a/solution.py
+++ b/solution.py
@@ -7,6 +7,18 @@
 MBLK = 128
 SPEAKERS = 4096
 reg_weight = 0.25
+
+
+def split_up(shard, dim, size):
+    shape = shard.shape
+    pieces = shard.reshape(*shape[:dim], size, shape[dim] // size, *shape[dim + 1 :])
+    return jnp.moveaxis(pieces, dim, 0)
+
+
+def laid_out(blocks, dim):
+    blocks = jnp.moveaxis(blocks, 0, dim)
+    dims = blocks.shape
+    return blocks.reshape(*dims[:dim], dims[dim] * dims[dim + 1], *dims[dim + 2 :])
 
 
 def complex_forward(plant, field_rows):
@@ -77,7 +89,14 @@
     weighted = (weights_flat[:, :, None] * pressure).astype(jnp.bfloat16)
     clipped = jnp.minimum(flat_labels, mic_units - 1)
     reply = weighted[clipped].reshape(devices, capacity, block_size, field_width)
-    returned = lax.all_to_all(reply, "spk", split_axis=0, concat_axis=0, tiled=True)
+    peers, place = (lax.axis_size("spk"), lax.axis_index("spk"))
+    blocks = split_up(reply, 0, peers)
+    done = [blocks[place]]
+    for lap in range(1, peers):
+        sent = blocks[place ^ lap]
+        done.append(lax.ppermute(sent, "spk", [(i, i ^ lap) for i in range(peers)]))
+    blocks = jnp.stack(done)[place ^ jnp.arange(peers)]
+    returned = laid_out(blocks, 0)
     tile_weighted = returned.reshape(devices * capacity, block_size, field_width)[position]
     back_field = complex_adjoint(plant, tile_weighted)
     unit_onehot = (local_unit[:, None] == jnp.arange(unit_count)[None, :]).astype(jnp.float32)

time: 213 us -> 240 us (1.13); the launches traced: 212 us -> 237 us
  blocking collectives: 64.1 us -> 24.6 us
  waiting for transfers between devices: 91.3 us -> 118 us
  starting transfers between devices: 16.8 us -> 36.8 us
  local copies, waits for them, and re-layouts: 19.7 us -> 37 us
    psum x1, blocking collectives: 64.1 us -> 24.6 us  [per_device(): bin_power = lax.psum(power_terms, 'spk')]
    ppermute x0 -> x15, waiting for transfers between devices: none -> 28 us  [per_device(): done.append(lax.ppermute(sent, 'spk', [(i, i ^ lap) for i in range(peers)]))]
    ppermute x0 -> x15, starting transfers between devices: none -> 24.6 us  [per_device(): done.append(lax.ppermute(sent, 'spk', [(i, i ^ lap) for i in range(peers)]))]
    unnamed x9 -> x23, local copies, waits for them, and re-layouts: 0.02 us -> 10.1 us
    all_to_all x1 -> x0, starting transfers between devices: 4.59 us -> none  [per_device(): lax.all_to_all(reply, 'spk', split_axis=0, concat_axis=0, tiled=True)]
    gather x0 -> x1, local copies, waits for them, and re-layouts: none -> 3.7 us  [per_device(): blocks = jnp.stack(done)[place ^ jnp.arange(peers)]]
    squeeze x0 -> x1, local copies, waits for them, and re-layouts: none -> 2.71 us  [per_device(): sent = blocks[place ^ lap]]
  transfers between devices with their start and end apart: 3 -> 17, of which waited for: 1 -> 9; matrix products, arithmetic and copies ran while one was open for 7% -> 11% of each run, Pallas kernels for 0% -> 0%
where the time goes in v1:
time: 240 us; the launch traced here: 237 us
  waiting for transfers between devices  118 us (49%)
  local copies, waits for them, and re-layouts  37 us (15%)
  starting transfers between devices  36.8 us (15%)
  blocking collectives  24.6 us (10%)
  other arithmetic  15.3 us (6%)
  matrix products  3.66 us (2%)
    all_to_all x1, waiting for transfers between devices, per_device(): lax.all_to_all(outgoing.reshape(devices, capacity, block_size, field_widt...  89.7 us
    ppermute x15, waiting for transfers between devices, per_device(): done.append(lax.ppermute(sent, 'spk', [(i, i ^ lap) for i in range(peers)]))  28 us
    ppermute x15, starting transfers between devices, per_device(): done.append(lax.ppermute(sent, 'spk', [(i, i ^ lap) for i in range(peers)]))  24.6 us
    psum x1, blocking collectives, per_device(): bin_power = lax.psum(power_terms, 'spk')  24.6 us
    unnamed x23, local copies, waits for them, and re-layouts  10.1 us
    scatter-add x1, other arithmetic, per_device(): jax.ops.segment_sum(arrived.reshape(devices * capacity, block_size, field...  8.78 us
    all_to_all x1, starting transfers between devices, per_device(): lax.all_to_all(labels.reshape(devices, capacity), 'spk', split_axis=0, co...  6.18 us
    all_to_all x1, starting transfers between devices, per_device(): lax.all_to_all(outgoing.reshape(devices, capacity, block_size, field_widt...  5.96 us
  transfers between devices with their start and end apart: 17, of which 9 were waited for; matrix products, arithmetic and copies ran while one was open for 11% of the time, Pallas kernels for 0%

profile of v1, /device:TPU:16, one launch (start us, length us, event | category | flops | bytes accessed | tf_op | source)
XLA Modules:
  0.0 236.5 jit_solution(10305390986525498439)
XLA Ops:
  0.0 0.8 fusion.16
  0.9 0.7 fusion.19
  1.7 0.8 gather_fusion.4
  2.5 0.7 scatter_custom_fusion
  3.2 0.7 all_to_all.9
  3.9 6.2 %all-to-all-start = ((s32[16,1,4]{2,1,0:T(1,128)}), s32[16,1,4]{2,1,0:T(1,128)S(1)}, u32[]{:S(2)}, u32[]{:S(2)}) async-start(s32[16,1,4]{2,1,0:T(1,128)} %bitcast.10), calls=%async_computation | async-start | bytes 16384 | tf_op jit(solution)/shard_map/all_to_all | solution.py:73
  10.0 0.9 convert_element_type.14
  11.0 0.7 gather_fusion
  11.7 0.7 convolution_bitcast_fusion.1
  12.6 0.2 pad_maximum_fusion
  12.8 1.7 copy.38
  14.5 2.5 %broadcast_in_dim.9 = f32[64,128,128]{2,1,0:T(8,128)} broadcast(f32[]{:T(128)} %constant.50.clone.1), dimensions={} | broadcast | bytes 4194308 | tf_op jit(solution)/shard_map/broadcast_in_dim | solution.py:68
  17.0 5.5 %scatter_fusion = f32[64,128,128]{2,1,0:T(8,128)} fusion(f32[64,128,128]{2,1,0:T(8,128)} %broadcast_in_dim.9, s32[26]{0:T(128)S(1)} %fusion.15, f32[26,128,128]{2,1,0:T(8,128)S(1)} %copy-done.1), kind=kCustom, calls=%fused_computation.6 | custom fusion | bytes 5111912 | tf_op jit(solution)/shard_map/scatter | solution.py:70
  22.4 6.0 %all-to-all-start.1 = ((f32[16,4,128,128]{3,2,1,0:T(8,128)}), f32[16,4,128,128]{3,2,1,0:T(8,128)}, u32[]{:S(2)}, u32[]{:S(2)}) async-start(f32[16,4,128,128]{3,2,1,0:T(8,128)} %bitcast.150), calls=%async_computation.1 | async-start | bytes 8388608 | tf_op jit(solution)/shard_map/all_to_all | solution.py:76
  28.4 1.5 multiply_reduce_fusion
  29.9 0.5 broadcast.216
  30.5 0.7 minimum_reduce_fusion
  31.4 89.7 %all-to-all-done.1 = f32[16,4,128,128]{3,2,1,0:T(8,128)} async-done(((f32[16,4,128,128]{3,2,1,0:T(8,128)}), f32[16,4,128,128]{3,2,1,0:T(8,128)}, u32[]{:S(2)}, u32[]{:S(2)}) %all-to-all-start.1) | async-done | bytes 4194336 | tf_op jit(solution)/shard_map/all_to_all | solution.py:76
  121.1 8.8 %scatter_fusion.1 = f32[9,128,128]{2,1,0:T(8,128)S(1)} fusion(f32[9,128,128]{2,1,0:T(8,128)S(1)} %broadcast_in_dim.8, s32[64]{0:T(128)S(1)} %reshape.142, f32[64,128,128]{2,1,0:T(8,128)} %bitcast.17), kind=kCustom, calls=%fused_computation.7 | custom fusion | flops 1048576 | bytes 12583168 | tf_op jit(solution)/shard_map/scatter-add | solution.py:84
  129.9 0.2 fusion.8
  130.1 2.1 gather_fusion.1
  132.3 2.7 %dynamic-slice_bitcast_fusion = (bf16[1,4,128,128]{3,2,1,0:T(8,128)(2,1)S(1)}, bf16[1,4,128,128]{3,2,1,0:T(8,128)(2,1)S(1)}, bf16[1,4,128,128]{3,2,1,0:T(8,128)(...) fusion(bf16[16,1,4,128,128]{4,3,2,0,1:T(8,128)(2,1)} %bitcast.1, ...), kind=kLoop, calls=%fused_computation.45 | loop fusion | bytes 4194368 | tf_op jit(solution)/shard_map/squeeze | solution.py:96
  135.6 24.6 %psum.7 = f32[1]{0:T(128)} all-reduce(f32[1]{0:T(128)} %bitcast.57), channel_id=1, replica_groups=mesh['band'=2,'spk'=16] {'spk'}, use_global_device_ids=true, to_apply=%region_5.6 | all-reduce | flops 1 | bytes 8 | tf_op jit(solution)/shard_map/psum | solution.py:58
  160.9 0.1 collective-permute-start.2
  161.0 7.1 %collective-permute-start.3 = (bf16[1,4,128,128]{3,2,1,0:T(8,128)(2,1)S(1)}, bf16[1,4,128,128]{3,2,1,0:T(8,128)(2,1)S(1)}, u32[]{:S(2)}, u32[]{:S(2)}) collective-permute-start(bf16[1,4,128,128]{3,2,1,0:T(8,128)(2,1)S(1)} %get-tuple-element.22), channel_id=1, source_target_pairs={{0,4},{1,5},{2,6},{3,7},{4,0},{5,1},{6,2},{7,3},{8,12},{9,13},{10,... | collective-permute-start | bytes 393224 | tf_op jit(solution)/shard_map/ppermute | solution.py:97
  168.2 1.3 collective-permute-start.5
  169.4 1.6 bitcast_dynamic-update-slice_fusion.14
  171.0 1.6 collective-permute-start.6
  172.6 0.7 bitcast_dynamic-update-slice_fusion.13
  173.2 4.0 %collective-permute-start.7 = (bf16[1,4,128,128]{3,2,1,0:T(8,128)(2,1)S(1)}, bf16[1,4,128,128]{3,2,1,0:T(8,128)(2,1)S(1)}, u32[]{:S(2)}, u32[]{:S(2)}) collective-permute-start(bf16[1,4,128,128]{3,2,1,0:T(8,128)(2,1)S(1)} %get-tuple-element.18), channel_id=1, source_target_pairs={{0,8},{1,9},{2,10},{3,11},{4,12},{5,13},{6,14},{7,15},{8,0},{9,1},... | collective-permute-start | bytes 393224 | tf_op jit(solution)/shard_map/ppermute | solution.py:97
  177.3 0.7 bitcast_dynamic-update-slice_fusion.12
  177.9 1.6 collective-permute-start.8
  179.5 0.7 bitcast_dynamic-update-slice_fusion.11
  180.2 2.2 collective-permute-start.9
  182.3 0.7 bitcast_dynamic-update-slice_fusion.10
  183.0 2.3 collective-permute-start.10
  185.3 0.7 bitcast_dynamic-update-slice_fusion.9
  185.9 0.3 collective-permute-start.11
  186.2 0.7 bitcast_dynamic-update-slice_fusion.8
  186.9 7.4 %collective-permute-done.7 = bf16[1,4,128,128]{3,2,1,0:T(8,128)(2,1)S(1)} collective-permute-done((bf16[1,4,128,128]{3,2,1,0:T(8,128)(2,1)S(1)}, bf16[1,4,128,128]{3,2,1,0:T(8,128)(2,1)S(1)}, u32[]{:S(2)}, u32[]{:S(2)}) %collective-permute-start.7) | collective-permute-done | bytes 131104 | tf_op jit(solution)/shard_map/ppermute | solution.py:97
  194.3 0.7 bitcast_dynamic-update-slice_fusion.7
  195.0 2.2 collective-permute-done.8
  197.1 3.6 %collective-permute-start.13 = (bf16[1,4,128,128]{3,2,1,0:T(8,128)(2,1)S(1)}, bf16[1,4,128,128]{3,2,1,0:T(8,128)(2,1)S(1)}, u32[]{:S(2)}, u32[]{:S(2)}) collective-permute-start(bf16[1,4,128,128]{3,2,1,0:T(8,128)(2,1)S(1)} %get-tuple-element.12), channel_id=1, source_target_pairs={{0,14},{1,15},{2,12},{3,13},{4,10},{5,11},{6,8},{7,9},{8,6},{9,7},... | collective-permute-start | bytes 393224 | tf_op jit(solution)/shard_map/ppermute | solution.py:97
  200.7 0.7 bitcast_dynamic-update-slice_fusion.6
  201.4 1.2 collective-permute-done.9
  202.6 0.5 collective-permute-start.14
  203.1 0.7 bitcast_dynamic-update-slice_fusion.5
  203.8 4.6 %collective-permute-done.10 = bf16[1,4,128,128]{3,2,1,0:T(8,128)(2,1)S(1)} collective-permute-done((bf16[1,4,128,128]{3,2,1,0:T(8,128)(2,1)S(1)}, bf16[1,4,128,128]{3,2,1,0:T(8,128)(2,1)S(1)}, u32[]{:S(2)}, u32[]{:S(2)}) %collective-permute-start.10) | collective-permute-done | bytes 131104 | tf_op jit(solution)/shard_map/ppermute | solution.py:97
  208.4 0.6 bitcast_dynamic-update-slice_fusion.4
  209.0 7.2 %collective-permute-done.11 = bf16[1,4,128,128]{3,2,1,0:T(8,128)(2,1)S(1)} collective-permute-done((bf16[1,4,128,128]{3,2,1,0:T(8,128)(2,1)S(1)}, bf16[1,4,128,128]{3,2,1,0:T(8,128)(2,1)S(1)}, u32[]{:S(2)}, u32[]{:S(2)}) %collective-permute-start.11) | collective-permute-done | bytes 131104 | tf_op jit(solution)/shard_map/ppermute | solution.py:97
  216.2 0.7 bitcast_dynamic-update-slice_fusion.3
  216.9 1.0 collective-permute-done.12
  217.9 0.7 bitcast_dynamic-update-slice_fusion.2
  218.5 3.8 %collective-permute-done.13 = bf16[1,4,128,128]{3,2,1,0:T(8,128)(2,1)S(1)} collective-permute-done((bf16[1,4,128,128]{3,2,1,0:T(8,128)(2,1)S(1)}, bf16[1,4,128,128]{3,2,1,0:T(8,128)(2,1)S(1)}, u32[]{:S(2)}, u32[]{:S(2)}) %collective-permute-start.13) | collective-permute-done | bytes 131104 | tf_op jit(solution)/shard_map/ppermute | solution.py:97
  222.4 0.7 bitcast_dynamic-update-slice_fusion.1
  223.0 0.5 collective-permute-done.14
  223.5 0.7 bitcast_dynamic-update-slice_fusion
  224.2 3.7 %gather_fusion.2 = bf16[16,4,128,128]{3,2,1,0:T(8,128)(2,1)} fusion(bf16[16,4,128,128]{3,2,1,0:T(8,128)(2,1)} %bitcast.153, s32[1024]{0:T(1024)S(1)} %pad_clamp_fusion.1), kind=kCustom, calls=%fused_computation.2 | custom fusion | bytes 4194368 | tf_op jit(solution)/shard_map/gather | solution.py:98
  227.9 2.3 gather_fusion.3
  230.2 0.7 convolution_bitcast_fusion
  231.0 0.1 fusion.2
  231.3 2.2 copy.42
  233.5 2.4 fusion.10
  235.9 0.7 copy_add_fusion
  (38 shorter events, 1.0 us)
Async XLA Ops:
  0.0 11.7 %copy-start = (bf16[26,2,128,128]{3,2,1,0:T(8,128)(2,1)S(1)}, bf16[26,2,128,128]{3,2,1,0:T(8,128)(2,1)}, u32[]{:S(2)}) copy-start(bf16[26,2,128,128]{3,2,1,0:T(8,128)(2,1)} %param.5) | copy-start | bytes 5111812
  3.9 18.6 %all-to-all-start = ((s32[16,1,4]{2,1,0:T(1,128)}), s32[16,1,4]{2,1,0:T(1,128)S(1)}, u32[]{:S(2)}, u32[]{:S(2)}) async-start(s32[16,1,4]{2,1,0:T(1,128)} %bitcast.10), calls=%async_computation | async-start | bytes 16384 | tf_op jit(solution)/shard_map/all_to_all | solution.py:73
  14.5 2.5 %copy-start.1 = (f32[26,128,128]{2,1,0:T(8,128)S(1)}, f32[26,128,128]{2,1,0:T(8,128)}, u32[]{:S(2)}) copy-start(f32[26,128,128]{2,1,0:T(8,128)} %copy.38) | copy-start | bytes 5111812
  22.4 98.6 %all-to-all-start.1 = ((f32[16,4,128,128]{3,2,1,0:T(8,128)}), f32[16,4,128,128]{3,2,1,0:T(8,128)}, u32[]{:S(2)}, u32[]{:S(2)}) async-start(f32[16,4,128,128]{3,2,1,0:T(8,128)} %bitcast.150), calls=%async_computation.1 | async-start | bytes 8388608 | tf_op jit(solution)/shard_map/all_to_all | solution.py:76
  121.1 8.8 %copy-start.3 = (f32[1,8,128]{2,1,0:T(8,128)S(1)}, f32[1,8,128]{2,1,0:T(8,128)}, u32[]{:S(2)}) copy-start(f32[1,8,128]{2,1,0:T(8,128)} %param.7) | copy-start | bytes 12292
  135.0 33.2 %collective-permute-start = (bf16[1,4,128,128]{3,2,1,0:T(8,128)(2,1)}, bf16[1,4,128,128]{3,2,1,0:T(8,128)(2,1)}, u32[]{:S(2)}, u32[]{:S(2)}) collective-permute-start(bf16[1,4,128,128]{3,2,1,0:T(8,128)(2,1)} %get-tuple-element.25), channel_id=1, source_target_pairs={{0,1},{1,0},{2,3},{3,2},{4,5},{5,4},{6,7},{7,6},{8,9},{9,8},{10,11... | collective-permute-start | bytes 393224 | tf_op jit(solution)/shard_map/ppermute | solution.py:97
  160.8 10.1 %collective-permute-start.1 = (bf16[1,4,128,128]{3,2,1,0:T(8,128)(2,1)S(1)}, bf16[1,4,128,128]{3,2,1,0:T(8,128)(2,1)S(1)}, u32[]{:S(2)}, u32[]{:S(2)}) collective-permute-start(bf16[1,4,128,128]{3,2,1,0:T(8,128)(2,1)S(1)} %get-tuple-element.24), channel_id=1, source_target_pairs={{0,2},{1,3},{2,0},{3,1},{4,6},{5,7},{6,4},{7,5},{8,10},{9,11},{10,... | collective-permute-start | bytes 393224 | tf_op jit(solution)/shard_map/ppermute | solution.py:97
  160.9 12.3 %collective-permute-start.2 = (bf16[1,4,128,128]{3,2,1,0:T(8,128)(2,1)S(1)}, bf16[1,4,128,128]{3,2,1,0:T(8,128)(2,1)S(1)}, u32[]{:S(2)}, u32[]{:S(2)}) collective-permute-start(bf16[1,4,128,128]{3,2,1,0:T(8,128)(2,1)S(1)} %get-tuple-element.23), channel_id=1, source_target_pairs={{0,3},{1,2},{2,1},{3,0},{4,7},{5,6},{6,5},{7,4},{8,11},{9,10},{10,... | collective-permute-start | bytes 393224 | tf_op jit(solution)/shard_map/ppermute | solution.py:97
  161.0 16.9 %collective-permute-start.3 = (bf16[1,4,128,128]{3,2,1,0:T(8,128)(2,1)S(1)}, bf16[1,4,128,128]{3,2,1,0:T(8,128)(2,1)S(1)}, u32[]{:S(2)}, u32[]{:S(2)}) collective-permute-start(bf16[1,4,128,128]{3,2,1,0:T(8,128)(2,1)S(1)} %get-tuple-element.22), channel_id=1, source_target_pairs={{0,4},{1,5},{2,6},{3,7},{4,0},{5,1},{6,2},{7,3},{8,12},{9,13},{10,... | collective-permute-start | bytes 393224 | tf_op jit(solution)/shard_map/ppermute | solution.py:97
  168.1 12.0 %collective-permute-start.4 = (bf16[1,4,128,128]{3,2,1,0:T(8,128)(2,1)S(1)}, bf16[1,4,128,128]{3,2,1,0:T(8,128)(2,1)S(1)}, u32[]{:S(2)}, u32[]{:S(2)}) collective-permute-start(bf16[1,4,128,128]{3,2,1,0:T(8,128)(2,1)S(1)} %get-tuple-element.21), channel_id=1, source_target_pairs={{0,5},{1,4},{2,7},{3,6},{4,1},{5,0},{6,3},{7,2},{8,13},{9,12},{10,... | collective-permute-start | bytes 393224 | tf_op jit(solution)/shard_map/ppermute | solution.py:97
  168.2 14.8 %collective-permute-start.5 = (bf16[1,4,128,128]{3,2,1,0:T(8,128)(2,1)S(1)}, bf16[1,4,128,128]{3,2,1,0:T(8,128)(2,1)S(1)}, u32[]{:S(2)}, u32[]{:S(2)}) collective-permute-start(bf16[1,4,128,128]{3,2,1,0:T(8,128)(2,1)S(1)} %get-tuple-element.20), channel_id=1, source_target_pairs={{0,6},{1,7},{2,4},{3,5},{4,2},{5,3},{6,0},{7,1},{8,14},{9,15},{10,... | collective-permute-start | bytes 393224 | tf_op jit(solution)/shard_map/ppermute | solution.py:97
  171.0 15.0 %collective-permute-start.6 = (bf16[1,4,128,128]{3,2,1,0:T(8,128)(2,1)S(1)}, bf16[1,4,128,128]{3,2,1,0:T(8,128)(2,1)S(1)}, u32[]{:S(2)}, u32[]{:S(2)}) collective-permute-start(bf16[1,4,128,128]{3,2,1,0:T(8,128)(2,1)S(1)} %get-tuple-element.19), channel_id=1, source_target_pairs={{0,7},{1,6},{2,5},{3,4},{4,3},{5,2},{6,1},{7,0},{8,15},{9,14},{10,... | collective-permute-start | bytes 393224 | tf_op jit(solution)/shard_map/ppermute | solution.py:97
  173.2 21.1 %collective-permute-start.7 = (bf16[1,4,128,128]{3,2,1,0:T(8,128)(2,1)S(1)}, bf16[1,4,128,128]{3,2,1,0:T(8,128)(2,1)S(1)}, u32[]{:S(2)}, u32[]{:S(2)}) collective-permute-start(bf16[1,4,128,128]{3,2,1,0:T(8,128)(2,1)S(1)} %get-tuple-element.18), channel_id=1, source_target_pairs={{0,8},{1,9},{2,10},{3,11},{4,12},{5,13},{6,14},{7,15},{8,0},{9,1},... | collective-permute-start | bytes 393224 | tf_op jit(solution)/shard_map/ppermute | solution.py:97
  177.9 19.2 %collective-permute-start.8 = (bf16[1,4,128,128]{3,2,1,0:T(8,128)(2,1)S(1)}, bf16[1,4,128,128]{3,2,1,0:T(8,128)(2,1)S(1)}, u32[]{:S(2)}, u32[]{:S(2)}) collective-permute-start(bf16[1,4,128,128]{3,2,1,0:T(8,128)(2,1)S(1)} %get-tuple-element.17), channel_id=1, source_target_pairs={{0,9},{1,8},{2,11},{3,10},{4,13},{5,12},{6,15},{7,14},{8,1},{9,0},... | collective-permute-start | bytes 393224 | tf_op jit(solution)/shard_map/ppermute | solution.py:97
  180.2 22.4 %collective-permute-start.9 = (bf16[1,4,128,128]{3,2,1,0:T(8,128)(2,1)S(1)}, bf16[1,4,128,128]{3,2,1,0:T(8,128)(2,1)S(1)}, u32[]{:S(2)}, u32[]{:S(2)}) collective-permute-start(bf16[1,4,128,128]{3,2,1,0:T(8,128)(2,1)S(1)} %get-tuple-element.16), channel_id=1, source_target_pairs={{0,10},{1,11},{2,8},{3,9},{4,14},{5,15},{6,12},{7,13},{8,2},{9,3},... | collective-permute-start | bytes 393224 | tf_op jit(solution)/shard_map/ppermute | solution.py:97
  183.0 25.4 %collective-permute-start.10 = (bf16[1,4,128,128]{3,2,1,0:T(8,128)(2,1)S(1)}, bf16[1,4,128,128]{3,2,1,0:T(8,128)(2,1)S(1)}, u32[]{:S(2)}, u32[]{:S(2)}) collective-permute-start(bf16[1,4,128,128]{3,2,1,0:T(8,128)(2,1)S(1)} %get-tuple-element.15), channel_id=1, source_target_pairs={{0,11},{1,10},{2,9},{3,8},{4,15},{5,14},{6,13},{7,12},{8,3},{9,2},... | collective-permute-start | bytes 393224 | tf_op jit(solution)/shard_map/ppermute | solution.py:97
  185.9 30.3 %collective-permute-start.11 = (bf16[1,4,128,128]{3,2,1,0:T(8,128)(2,1)S(1)}, bf16[1,4,128,128]{3,2,1,0:T(8,128)(2,1)S(1)}, u32[]{:S(2)}, u32[]{:S(2)}) collective-permute-start(bf16[1,4,128,128]{3,2,1,0:T(8,128)(2,1)S(1)} %get-tuple-element.14), channel_id=1, source_target_pairs={{0,12},{1,13},{2,14},{3,15},{4,8},{5,9},{6,10},{7,11},{8,4},{9,5},... | collective-permute-start | bytes 393224 | tf_op jit(solution)/shard_map/ppermute | solution.py:97
  194.3 23.6 %collective-permute-start.12 = (bf16[1,4,128,128]{3,2,1,0:T(8,128)(2,1)S(1)}, bf16[1,4,128,128]{3,2,1,0:T(8,128)(2,1)S(1)}, u32[]{:S(2)}, u32[]{:S(2)}) collective-permute-start(bf16[1,4,128,128]{3,2,1,0:T(8,128)(2,1)S(1)} %get-tuple-element.13), channel_id=1, source_target_pairs={{0,13},{1,12},{2,15},{3,14},{4,9},{5,8},{6,11},{7,10},{8,5},{9,4},... | collective-permute-start | bytes 393224 | tf_op jit(solution)/shard_map/ppermute | solution.py:97
  197.1 25.2 %collective-permute-start.13 = (bf16[1,4,128,128]{3,2,1,0:T(8,128)(2,1)S(1)}, bf16[1,4,128,128]{3,2,1,0:T(8,128)(2,1)S(1)}, u32[]{:S(2)}, u32[]{:S(2)}) collective-permute-start(bf16[1,4,128,128]{3,2,1,0:T(8,128)(2,1)S(1)} %get-tuple-element.12), channel_id=1, source_target_pairs={{0,14},{1,15},{2,12},{3,13},{4,10},{5,11},{6,8},{7,9},{8,6},{9,7},... | collective-permute-start | bytes 393224 | tf_op jit(solution)/shard_map/ppermute | solution.py:97
  202.6 20.9 %collective-permute-start.14 = (bf16[1,4,128,128]{3,2,1,0:T(8,128)(2,1)S(1)}, bf16[1,4,128,128]{3,2,1,0:T(8,128)(2,1)S(1)}, u32[]{:S(2)}, u32[]{:S(2)}) collective-permute-start(bf16[1,4,128,128]{3,2,1,0:T(8,128)(2,1)S(1)} %get-tuple-element.11), channel_id=1, source_target_pairs={{0,15},{1,14},{2,13},{3,12},{4,11},{5,10},{6,9},{7,8},{8,7},{9,6},... | collective-permute-start | bytes 393224 | tf_op jit(solution)/shard_map/ppermute | solution.py:97
  231.3 4.6 %copy-start.2 = (f32[2,128,128]{2,1,0:T(8,128)S(1)}, f32[2,128,128]{2,1,0:T(8,128)}, u32[]{:S(2)}) copy-start(f32[2,128,128]{2,1,0:T(8,128)} %param.4) | copy-start | bytes 393220
